TPU v7x, 32 devices: a whole 2x2x4 slice. The times are simulated.
32 devices in a mesh: grp: 4 (over y, x), blk: 8 (over z, core).
Axes of the slice: x: 2, y: 2, z: 4, core: 2. Of those that a mesh axis runs over, the one named last changes fastest.
Arguments:
- voltages: bfloat16 [4096, 188416], P(('blk', 'grp')), may hold values from -6 to 6
- filter_taps: float32 [8, 8192], replicated, may hold values from -0.0234375 to 0.0234375
- channel_index: int32 [16], replicated, may hold values from 0 to 4095
- antenna_slot_order: int32 [2048], replicated, may hold values from 0 to 2047, each once
Outputs:
- visibilities: bfloat16 [16, 4096, 2, 4096], P('grp', 'blk')
All inputs are finite; a program needn't handle non-finite values.
Results may differ from a plain program's by a relative error of at most 0.0065.
Values sent between devices are 32-bit elements; how exact they have to be, the bound alone decides.
No kernel may reach another device: no remote copies, remote signals or barrier semaphores. Data moves between devices by JAX's collectives and lax.ppermute only.
A program may use at most 192 MiB of HBM per device.

v0:
```python
import math
import jax
import jax.numpy as jnp
from jax import lax
from jax.sharding import PartitionSpec as P


def phase_table(channel_index, fft_length):
    samples_idx = jnp.arange(fft_length, dtype=jnp.int32)
    phase = samples_idx[:, None] * channel_index[None, :] % fft_length
    angle = phase.astype(jnp.float32) * jnp.float32(2.0 * math.pi / fft_length)
    return jnp.concatenate([jnp.cos(angle), -jnp.sin(angle)], axis=1).astype(jnp.bfloat16)


def channelize(voltages, filter_taps, channel_index):
    tap_count, fft_length = filter_taps.shape
    row_count = voltages.shape[0]
    frame_count = voltages.shape[1] // fft_length
    spectra = frame_count - tap_count + 1
    blocked = voltages.reshape(row_count, frame_count, fft_length)
    filtered = jnp.zeros((row_count, spectra, fft_length), jnp.float32)
    for tap_index in range(tap_count):
        filtered = filtered + filter_taps[tap_index][None, None, :] * blocked[
            :, tap_index : tap_index + spectra, :
        ].astype(jnp.float32)
    twiddle = phase_table(channel_index, fft_length)
    spectrum = jnp.dot(
        filtered.astype(jnp.bfloat16).reshape(row_count * spectra, fft_length),
        twiddle,
        preferred_element_type=jnp.float32,
    )
    chan_count = channel_index.shape[0]
    return (
        spectrum.reshape(row_count, spectra, 2, chan_count)
        .transpose(3, 2, 1, 0)
        .reshape(chan_count, 2 * spectra, row_count)
    )


def column_index(antenna_slot_order):
    count = antenna_slot_order.shape[0]
    inverse = (
        jnp.zeros((count,), jnp.int32)
        .at[antenna_slot_order]
        .set(jnp.arange(count, dtype=jnp.int32))
    )
    column_entry = jnp.arange(2 * count, dtype=jnp.int32)
    return 2 * inverse[column_entry // 2] + column_entry % 2


def stacked_rows(block):
    half = block.shape[1] // 2
    turned = jnp.concatenate([block[:, half:], -block[:, :half]], axis=1)
    return jnp.stack([block, turned], axis=1)


def correlate(lhs, cols):
    return jnp.einsum(
        "cpkr,ckn->crpn",
        lhs,
        cols,
        precision=lax.Precision.HIGHEST,
        preferred_element_type=jnp.float32,
    )


def per_device(voltages, filter_taps, channel_index, antenna_slot_order):
    local = channelize(voltages, filter_taps, channel_index)
    scale = jnp.float32(1.0 / (local.shape[1] // 2))
    columns = column_index(antenna_slot_order)
    turned = lax.all_to_all(local, "grp", split_axis=0, concat_axis=2, tiled=True)
    lhs = stacked_rows(turned)
    everything = lax.all_gather(turned, "blk", axis=2, tiled=True)
    ordered = jnp.take(everything, columns, axis=2)
    result = (correlate(lhs, ordered) * scale).astype(jnp.bfloat16)
    return result


def solution(mesh):
    in_specs = (P(("blk", "grp"), None), P(), P(), P())
    out_specs = P("grp", "blk", None, None)
    return jax.shard_map(
        per_device, mesh=mesh, in_specs=in_specs, out_specs=out_specs, check_vma=False
    )
```

profile of v0, /device:TPU:0, one launch (start us, length us, event | category | flops | bytes accessed | tf_op | source)
XLA Modules:
  0.0 413.1 jit_solution(9023769274649659987)
XLA Ops:
  6.5 0.0 all-gather.2.cloned.1.call-start
  6.5 2.3 fusion.25
  8.9 3.2 cosine_convert_fusion
  12.1 62.3 %copy.14 = bf16[128,188416]{0,1:T(8,128)(2,1)} copy(bf16[128,188416]{1,0:T(8,128)(2,1)} %param.4) | data formatting | bytes 96468992 | tf_op args[0]
  74.4 0.0 copy-start
  74.4 91.6 %fusion.4 = f32[16,2,16,128]{3,0,1,2:T(8,128)S(1)} fusion(bf16[2,16,8192,1]{2,1,0,3:T(8,128)(2,1)S(1)} %bitcast.55, bf16[128,23,8192]{0,2,1:T(8,128)(2,1)} %bitcast.49, f32[8192]{0:T(1024)S(1)} %bitcast.65, f32[8192]{0:T(1024)S(1)} %bitcast.66, f32[8192]{0:T(1024)S(1)} %bitcast.60, f32[8192]{0:T(1024)S(1)} %bitcast.61, f32[8192]{0:T(1024)S(1)} %bitcast.62, ...), kind=kOutput, calls=%fused_computation.10 | convolution fusion | flops 1476395008 | bytes 269484032 | tf_op jit(solution)/shard_map/dot_general | solution.py:27
  166.0 0.2 copy.16
  166.2 10.7 %all_to_all.18 = f32[16,32,128]{2,1,0:T(8,128)S(1)} all-to-all(f32[16,32,128]{2,1,0:T(8,128)S(1)} %bitcast.54), channel_id=1, replica_groups=mesh['grp'=4,'blk'=8] {'grp'}, dimensions={0} | all-to-all | bytes 524288 | tf_op jit(solution)/shard_map/all_to_all | solution.py:71
  176.9 0.7 copy.33
  177.6 0.0 all-gather.2.cloned.1.call-update
  177.7 0.0 copy-done
  177.7 8.2 %scatter_custom_fusion = s32[2048]{0:T(1024)S(1)} fusion(s32[2048]{0:T(1024)S(1)} %compare_select_fusion.3, s32[2048]{0:T(1024)S(1)} %iota.16, s32[]{:T(128)} %constant.59.clone.1), kind=kCustom, calls=%fused_computation.49 | custom fusion | bytes 8196 | tf_op jit(solution)/shard_map/scatter | solution.py:45
  186.0 23.0 %gather_fusion = s32[4096]{0:T(1024)S(1)} fusion(s32[2048]{0:T(1024)S(1)} %scatter_custom_fusion, s32[4096]{0:T(1024)S(1)} %broadcast_clamp_fusion.1), kind=kCustom, calls=%fused_computation | custom fusion | bytes 49152 | tf_op jit(solution)/shard_map/gather | solution.py:48
  209.1 0.2 copy.17
  209.3 0.1 stack.9
  209.4 1.0 fusion.24
  210.4 0.0 all-gather.2.cloned.1.call-done
  210.4 7.2 %copy.18 = f32[4,32,4096]{1,0,2:T(4,128)} copy(f32[4,32,4096]{2,1,0:T(8,128)} %all-gather.2.cloned.1.call-done) | data formatting | bytes 4194304 | tf_op jit(solution)/shard_map/all_gather | solution.py:73
  217.6 33.3 %gather_fusion.1 = f32[4096,4,32]{2,1,0:T(4,128)} fusion(f32[4,32,4096]{1,0,2:T(4,128)} %copy.18, s32[4096]{0:T(1024)S(1)} %broadcast_clamp_fusion), kind=kCustom, calls=%fused_computation.1 | custom fusion | bytes 4210688 | tf_op jit(solution)/shard_map/jit(_take)/gather | solution.py:74
  251.0 16.4 %select_bitcast_fusion = f32[4,32,4096,1]{1,0,2,3:T(4,128)S(1)} fusion(f32[4096,4,32]{2,1,0:T(4,128)} %gather_fusion.1, pred[4096]{0:T(1024)(128)(4,1)S(1)} %compare_and_fusion), kind=kLoop, calls=%fused_computation.9 | loop fusion | flops 524288 | bytes 4198400 | tf_op jit(solution)/shard_map/jit(_take)/select_n | solution.py:74
  267.3 57.2 %fusion.2 = bf16[4,512,2,4096]{1,3,2,0:T(8,128)(2,1)} fusion(f32[4,32,4096,1]{1,0,2,3:T(4,128)S(1)} %select_bitcast_fusion, f32[4,1,32,512]{3,2,1,0:T(8,128)S(1)} %maximum_bitcast_fusion, f32[4,1,32,512]{3,2,1,0:T(8,128)S(1)} %stack.9), kind=kOutput, calls=%fused_computation.7 | convolution fusion | flops 6476136448 | bytes 36175872 | tf_op jit(solution)/shard_map/cpkr,ckn->crpn/dot_general | solution.py:58
  324.5 81.8 %copy.21 = bf16[4,512,2,4096]{3,2,1,0:T(2,128)(2,1)} copy(bf16[4,512,2,4096]{1,3,2,0:T(8,128)(2,1)} %fusion.2) | data formatting | bytes 67108864 | tf_op jit(solution)/shard_map/convert_element_type | solution.py:75
  (10 shorter events, 0.1 us)
Async XLA Ops:
  6.5 203.9 %all-gather.2.cloned.1.call-start = ((), (), s32[]{:S(2)}) async-start(), calls=%async_computation.1 | async-start | bytes 2359296 | tf_op jit(solution)/shard_map/all_gather | solution.py:73
  74.4 103.2 %copy-start = (s32[2048]{0:T(1024)S(1)}, s32[2048]{0:T(1024)}, u32[]{:S(2)}) copy-start(s32[2048]{0:T(1024)} %param.7) | copy-start | bytes 24580
Sparse Core Ops, SparseCore 0:
  177.8 28.8 all-gather.1
where the time goes:
time: 417 us; the launch traced here: 413 us
  local copies, waits for them, and re-layouts  219 us (53%)
  matrix products  149 us (36%)
  other arithmetic  20.7 us (5%)
  between operations  13.6 us (3%)
  blocking collectives  10.7 us (3%)
    dot_general x1, matrix products, channelize(): jnp.dot(filtered.astype(jnp.bfloat16).reshape(row_count * spectra, fft_le...  91.6 us
    convert_element_type x1, local copies, waits for them, and re-layouts, per_device(): result = (correlate(lhs, ordered) * scale).astype(jnp.bfloat16)  81.8 us
    unnamed x3, local copies, waits for them, and re-layouts  62.3 us
    dot_general x1, matrix products, correlate(): jnp.einsum('cpkr,ckn->crpn', lhs, cols, precision=lax.Precision.HIGHEST,...  57.2 us
    gather x1, local copies, waits for them, and re-layouts, per_device(): ordered = jnp.take(everything, columns, axis=2)  33.3 us
    gather x1, local copies, waits for them, and re-layouts, column_index(): return 2 * inverse[column_entry // 2] + column_entry % 2  23 us
    select_n x2, other arithmetic, per_device(): ordered = jnp.take(everything, columns, axis=2)  16.4 us
    all_to_all x1, blocking collectives, per_device(): lax.all_to_all(local, 'grp', split_axis=0, concat_axis=2, tiled=True)  10.7 us
  transfers between devices with their start and end apart: 1, of which 0 were waited for; matrix products, arithmetic and copies ran while one was open for 8% of the time, Pallas kernels for 0%

commit v1 on v0

--- a/solution.py
+++ b/solution.py
@@ -3,6 +3,18 @@
 import jax.numpy as jnp
 from jax import lax
 from jax.sharding import PartitionSpec as P
+
+
+def sent_to_each(x, axis, split, join):
+    ways, here = (lax.axis_size(axis), lax.axis_index(axis))
+    width = x.shape[split] // ways
+    turned = jnp.roll(x, -here * width, axis=split)
+    got = [lax.slice_in_dim(turned, 0, width, axis=split)]
+    for far in range(1, ways):
+        sent = lax.slice_in_dim(turned, far * width, (far + 1) * width, axis=split)
+        got.append(lax.ppermute(sent, axis, [(d, (d + far) % ways) for d in range(ways)]))
+    line = jnp.concatenate(got[::-1], axis=join)
+    return jnp.roll(line, (here + 1) * got[0].shape[join], axis=join)
 
 
 def phase_table(channel_index, fft_length):
@@ -68,7 +80,7 @@
     local = channelize(voltages, filter_taps, channel_index)
     scale = jnp.float32(1.0 / (local.shape[1] // 2))
     columns = column_index(antenna_slot_order)
-    turned = lax.all_to_all(local, "grp", split_axis=0, concat_axis=2, tiled=True)
+    turned = sent_to_each(local, "grp", 0, 2)
     lhs = stacked_rows(turned)
     everything = lax.all_gather(turned, "blk", axis=2, tiled=True)
     ordered = jnp.take(everything, columns, axis=2)

time: 417 us -> 409 us (0.981)
  blocking collectives: 10.7 us -> 0 us
  starting transfers between devices: 0.01 us -> 5.08 us
  local copies, waits for them, and re-layouts: 219 us -> 214 us
    all_to_all x1 -> x0, blocking collectives: 10.7 us -> none  [per_device(): lax.all_to_all(local, 'grp', split_axis=0, concat_axis=2, tiled=True)]
    ppermute x0 -> x3, starting transfers between devices: none -> 5.07 us  [sent_to_each(): lax.ppermute(sent, axis, [(d, (d + far) % ways) for d in range(ways)])]
    unnamed x3 -> x10, local copies, waits for them, and re-layouts: 62.3 us -> 57.4 us
  transfers between devices with their start and end apart: 1 -> 4, of which waited for: 0 -> 3; matrix products, arithmetic and copies ran while one was open for 8% -> 8% of each run, Pallas kernels for 0% -> 0%
where the time goes in v1:
time: 409 us; the launch traced here: 406 us
  local copies, waits for them, and re-layouts  214 us (52%)
  matrix products  149 us (36%)
  other arithmetic  19.7 us (5%)
  between operations  13.6 us (3%)
  starting transfers between devices  5.08 us (1%)
  waiting for transfers between devices  4.09 us (1%)
    dot_general x1, matrix products, channelize(): jnp.dot(filtered.astype(jnp.bfloat16).reshape(row_count * spectra, fft_le...  91.6 us
    convert_element_type x1, local copies, waits for them, and re-layouts, per_device(): result = (correlate(lhs, ordered) * scale).astype(jnp.bfloat16)  81.8 us
    unnamed x10, local copies, waits for them, and re-layouts  57.4 us
    dot_general x1, matrix products, correlate(): jnp.einsum('cpkr,ckn->crpn', lhs, cols, precision=lax.Precision.HIGHEST,...  57.2 us
    gather x1, local copies, waits for them, and re-layouts, per_device(): ordered = jnp.take(everything, columns, axis=2)  33.4 us
    gather x1, local copies, waits for them, and re-layouts, column_index(): return 2 * inverse[column_entry // 2] + column_entry % 2  23 us
    select_n x2, other arithmetic, per_device(): ordered = jnp.take(everything, columns, axis=2)  16.4 us
    scatter x1, local copies, waits for them, and re-layouts, column_index(): inverse = jnp.zeros((count,), jnp.int32).at[antenna_slot_order].set(jnp.a...  8.23 us
  transfers between devices with their start and end apart: 4, of which 3 were waited for; matrix products, arithmetic and copies ran while one was open for 8% of the time, Pallas kernels for 0%

profile of v1, /device:TPU:0, one launch (start us, length us, event | category | flops | bytes accessed | tf_op | source)
XLA Modules:
  0.0 405.5 jit_solution(4017176406976142855)
XLA Ops:
  6.5 0.0 all-gather.2.cloned.1.call-start
  6.5 2.3 fusion.26
  8.9 3.2 cosine_convert_fusion
  12.1 57.3 %copy.14 = bf16[128,188416]{0,1:T(8,128)(2,1)} copy(bf16[128,188416]{1,0:T(8,128)(2,1)} %param.4) | data formatting | bytes 96468992 | tf_op args[0]
  69.4 0.0 copy-start
  69.4 91.6 %fusion.4 = f32[16,2,16,128]{3,0,1,2:T(8,128)S(1)} fusion(bf16[2,16,8192,1]{2,1,0,3:T(8,128)(2,1)S(1)} %bitcast.46, bf16[128,23,8192]{0,2,1:T(8,128)(2,1)} %bitcast.44, f32[8192]{0:T(1024)S(1)} %bitcast.56, f32[8192]{0:T(1024)S(1)} %bitcast.57, f32[8192]{0:T(1024)S(1)} %bitcast.51, f32[8192]{0:T(1024)S(1)} %bitcast.52, f32[8192]{0:T(1024)S(1)} %bitcast.53, ...), kind=kOutput, calls=%fused_computation.10 | convolution fusion | flops 1476395008 | bytes 269484032 | tf_op jit(solution)/shard_map/dot_general | solution.py:39
  161.0 0.2 copy.16
  161.2 0.1 fusion.16
  161.3 4.0 collective-permute-start
  165.2 0.0 collective-permute-start.2
  165.2 1.1 collective-permute-start.1
  166.3 1.0 collective-permute-done
  167.3 2.4 collective-permute-done.1
  169.7 0.7 collective-permute-done.2
  170.5 0.7 constant_dynamic-slice_fusion.1
  171.2 0.0 all-gather.2.cloned.1.call-update
  171.2 0.0 copy-done
  171.3 8.2 %scatter_custom_fusion = s32[2048]{0:T(1024)S(1)} fusion(s32[2048]{0:T(1024)S(1)} %compare_select_fusion.3, s32[2048]{0:T(1024)S(1)} %iota.16, s32[]{:T(128)} %constant.100.clone.1), kind=kCustom, calls=%fused_computation.59 | custom fusion | bytes 8196 | tf_op jit(solution)/shard_map/scatter | solution.py:57
  179.5 23.0 %gather_fusion = s32[4096]{0:T(1024)S(1)} fusion(s32[2048]{0:T(1024)S(1)} %scatter_custom_fusion, s32[4096]{0:T(1024)S(1)} %broadcast_clamp_fusion.1), kind=kCustom, calls=%fused_computation | custom fusion | bytes 49152 | tf_op jit(solution)/shard_map/gather | solution.py:60
  202.8 0.0 all-gather.2.cloned.1.call-done
  202.8 7.2 %copy.17 = f32[4,32,4096]{1,0,2:T(4,128)} copy(f32[4,32,4096]{2,1,0:T(8,128)} %all-gather.2.cloned.1.call-done) | data formatting | bytes 4194304 | tf_op jit(solution)/shard_map/all_gather | solution.py:85
  210.0 33.4 %gather_fusion.1 = f32[4096,4,32]{2,1,0:T(4,128)} fusion(f32[4,32,4096]{1,0,2:T(4,128)} %copy.17, s32[4096]{0:T(1024)S(1)} %broadcast_clamp_fusion), kind=kCustom, calls=%fused_computation.1 | custom fusion | bytes 4210688 | tf_op jit(solution)/shard_map/jit(_take)/gather | solution.py:86
  243.4 16.4 %select_bitcast_fusion = f32[4,32,4096,1]{1,0,2,3:T(4,128)S(1)} fusion(f32[4096,4,32]{2,1,0:T(4,128)} %gather_fusion.1, pred[4096]{0:T(1024)(128)(4,1)S(1)} %compare_and_fusion), kind=kLoop, calls=%fused_computation.9 | loop fusion | flops 524288 | bytes 4198400 | tf_op jit(solution)/shard_map/jit(_take)/select_n | solution.py:86
  259.7 57.2 %fusion.2 = bf16[4,512,2,4096]{1,3,2,0:T(8,128)(2,1)} fusion(f32[4,32,4096,1]{1,0,2,3:T(4,128)S(1)} %select_bitcast_fusion, f32[4,1,32,512]{3,2,1,0:T(8,128)S(1)} %maximum_bitcast_fusion, f32[4,1,32,512]{3,2,1,0:T(8,128)S(1)} %fusion.28), kind=kOutput, calls=%fused_computation.7 | convolution fusion | flops 6476136448 | bytes 36175872 | tf_op jit(solution)/shard_map/cpkr,ckn->crpn/dot_general | solution.py:70
  316.9 81.8 %copy.19 = bf16[4,512,2,4096]{3,2,1,0:T(2,128)(2,1)} copy(bf16[4,512,2,4096]{1,3,2,0:T(8,128)(2,1)} %fusion.2) | data formatting | bytes 67108864 | tf_op jit(solution)/shard_map/convert_element_type | solution.py:87
  (21 shorter events, 0.3 us)
Async XLA Ops:
  6.5 196.2 %all-gather.2.cloned.1.call-start = ((), (), s32[]{:S(2)}) async-start(), calls=%async_computation | async-start | bytes 2359296 | tf_op jit(solution)/shard_map/all_gather | solution.py:85
  69.4 101.8 %copy-start = (s32[2048]{0:T(1024)S(1)}, s32[2048]{0:T(1024)}, u32[]{:S(2)}) copy-start(s32[2048]{0:T(1024)} %param.7) | copy-start | bytes 24580
  161.3 6.0 %collective-permute-start = (f32[4,32,128]{2,1,0:T(8,128)S(1)}, f32[4,32,128]{2,1,0:T(8,128)S(1)}, u32[]{:S(2)}, u32[]{:S(2)}) collective-permute-start(f32[4,32,128]{2,1,0:T(8,128)S(1)} %get-tuple-element.9), channel_id=1, source_target_pairs={{0,24},{8,0},{16,8},{24,16},{1,25},{9,1},{17,9},{25,17},{2,26},{10... | collective-permute-start | bytes 196616 | tf_op jit(solution)/shard_map/ppermute | solution.py:15
  165.2 5.2 %collective-permute-start.2 = (f32[4,32,128]{2,1,0:T(8,128)S(1)}, f32[4,32,128]{2,1,0:T(8,128)S(1)}, u32[]{:S(2)}, u32[]{:S(2)}) collective-permute-start(f32[4,32,128]{2,1,0:T(8,128)S(1)} %get-tuple-element.7), channel_id=1, source_target_pairs={{0,8},{8,16},{16,24},{24,0},{1,9},{9,17},{17,25},{25,1},{2,10},{10... | collective-permute-start | bytes 196616 | tf_op jit(solution)/shard_map/ppermute | solution.py:15
  165.2 4.4 %collective-permute-start.1 = (f32[4,32,128]{2,1,0:T(8,128)S(1)}, f32[4,32,128]{2,1,0:T(8,128)S(1)}, u32[]{:S(2)}, u32[]{:S(2)}) collective-permute-start(f32[4,32,128]{2,1,0:T(8,128)S(1)} %get-tuple-element.8), channel_id=1, source_target_pairs={{0,16},{8,24},{16,0},{24,8},{1,17},{9,25},{17,1},{25,9},{2,18},{10... | collective-permute-start | bytes 196616 | tf_op jit(solution)/shard_map/ppermute | solution.py:15
Sparse Core Ops, SparseCore 0:
  171.4 29.9 all-gather.1
